TPU v7x, 32 devices: a whole 2x2x4 slice. The times are simulated.
32 devices in a mesh: seq: 16 (over z, y, core), mp: 2 (over x).
Axes of the slice: x: 2, y: 2, z: 4, core: 2. Of those that a mesh axis runs over, the one named last changes fastest.
Arguments:
- tokens: bfloat16 [4096, 2048], P('seq'), may hold values from -25 to 25
- lengths: int32 [32], replicated, may hold values from 1 to 1024, 4096 in all
- prefix_cache: bfloat16 [4, 2048, 512], P(None, 'seq'), may hold values from -1000 to 1000
- attn_gain: bfloat16 [2048], replicated, may hold values from 0.25 to 1.75
- w_query: bfloat16 [2048, 2048], P(None, 'mp'), may hold values from -0.25 to 0.25
- w_keyval: bfloat16 [2048, 512], replicated, may hold values from -0.125 to 0.125
- w_out: bfloat16 [2048, 2048], P('mp'), may hold values from -0.25 to 0.25
- final_gain: bfloat16 [2048], replicated, may hold values from 0.25 to 1.75
- w_head: bfloat16 [2048, 32000], P(None, ('seq', 'mp')), may hold values from -0.4375 to 0.4375
Outputs:
- hidden: bfloat16 [4096, 2048], P('seq', 'mp')
- suffix_cache: bfloat16 [4096, 512], P('seq')
- last_normed: bfloat16 [32, 2048], replicated
- greatest: float32 [32], replicated
Inputs may be any that keep to these rules, and one draw needn't show every extreme that they name: The lengths sum to 4096 and one of them equals 1024.
All inputs are finite; a program needn't handle non-finite values.
Results may differ from a plain program's by a relative error of at most 0.013.
Values may be sent and summed in bfloat16 or wider, within the bound.
No kernel may reach another device: no remote copies, remote signals or barrier semaphores. Data moves between devices by JAX's collectives and lax.ppermute only.
A program may use at most 64 MiB of HBM per device.

v0:
```python
import math
import jax
import jax.numpy as jnp
from jax import lax
from jax.sharding import PartitionSpec as P

QH = 32
KVH = 4
HD = 64
G = 4
RPG = 8
P_SIZE = 2048
MOST = 1024
PREFIX_CHUNK = 512
epsilon = 1e-05


def rotate(source, places, head_count):
    half_dim = HD // 2
    row_count = source.shape[0]
    reshaped = source.reshape(row_count, head_count, HD)
    frequency = 10000.0 ** (-(jnp.arange(half_dim, dtype=jnp.float32) * 2.0 / HD))
    angles = places.astype(jnp.float32)[:, None] * frequency[None, :]
    cos_table = jnp.cos(angles)[:, None, :]
    sine_table = jnp.sin(angles)[:, None, :]
    leading = reshaped[..., :half_dim]
    second = reshaped[..., half_dim:]
    joined = jnp.concatenate(
        [leading * cos_table - second * sine_table, second * cos_table + leading * sine_table], -1
    )
    return joined.reshape(row_count, head_count * HD)


def attend(running, queries, kv_block, allowed):
    old_max, old_sum, numerator = running
    half_width = kv_block.shape[1] // 2
    kv_heads = queries.shape[1]
    key_rows = kv_block[:, :half_width].reshape(kv_block.shape[0], kv_heads, HD)
    val_rows = kv_block[:, half_width:].reshape(kv_block.shape[0], kv_heads, HD)
    scores = jnp.einsum("qgrd,ngd->grqn", queries, key_rows, preferred_element_type=jnp.float32) * (
        1.0 / math.sqrt(HD)
    )
    scores = jnp.where(allowed[None, None], scores, -jnp.inf)
    new_max = jnp.maximum(old_max, jnp.max(scores, -1))
    factor = jnp.exp(old_max - new_max)
    weights = jnp.exp(scores - new_max[..., None])
    new_sum = old_sum * factor + jnp.sum(weights, -1)
    numerator = numerator * factor[..., None] + jnp.einsum(
        "grqn,ngd->grqd", weights.astype(jnp.bfloat16), val_rows, preferred_element_type=jnp.float32
    )
    return (new_max, new_sum, numerator)


def shifted_back(block, axis, distance):
    count = lax.axis_size(axis)
    route = [(i, i + distance) for i in range(count - distance)]
    return lax.ppermute(block, axis, route)


def per_device(
    tokens, lengths, prefix_cache, attn_gain, w_query, w_keyval, w_out, final_gain, w_head
):
    token_rows = tokens.shape[0]
    model_width = tokens.shape[1]
    seq_devices = lax.axis_size("seq")
    seq_index = lax.axis_index("seq")
    mp_index = lax.axis_index("mp")
    part_width = model_width // lax.axis_size("mp")
    query_heads = w_query.shape[1] // HD
    group_size = QH // KVH
    kv_heads = max(1, query_heads // group_size)
    repeat_count = query_heads // kv_heads
    kv_first = mp_index * query_heads // group_size
    kv_width = KVH * HD
    request_count = lengths.shape[0]
    back_blocks = min(seq_devices - 1, -(-(MOST - 1) // token_rows))
    own_prefix = jnp.concatenate(
        [
            lax.dynamic_slice_in_dim(prefix_cache, kv_first * HD, kv_heads * HD, 2),
            lax.dynamic_slice_in_dim(prefix_cache, kv_width + kv_first * HD, kv_heads * HD, 2),
        ],
        2,
    )
    prefix_rows = own_prefix.shape[1]
    block_width = own_prefix.shape[2]
    all_prefix = lax.all_gather(own_prefix, "seq", axis=0)
    activations = tokens.astype(jnp.float32)
    normed = (
        activations
        * lax.rsqrt(jnp.mean(activations * activations, -1, keepdims=True) + epsilon)
        * attn_gain.astype(jnp.float32)
    ).astype(jnp.bfloat16)
    request_end = jnp.cumsum(lengths)
    starts = request_end - lengths
    position = seq_index * token_rows + jnp.arange(token_rows, dtype=jnp.int32)
    request = jnp.sum((position[:, None] >= request_end[None, :]).astype(jnp.int32), 1)
    request_table = request[:, None] == jnp.arange(request_count, dtype=jnp.int32)[None, :]
    offset = position - jnp.sum(jnp.where(request_table, starts[None, :], 0), 1)
    group_of = request // RPG
    keyval = jnp.dot(normed, w_keyval, preferred_element_type=jnp.float32)
    key_rows = rotate(keyval[:, :kv_width], P_SIZE + offset, KVH).astype(jnp.bfloat16)
    val_rows = keyval[:, kv_width:].astype(jnp.bfloat16)
    suffix_cache = jnp.concatenate([key_rows, val_rows], 1)
    own_suffix = jnp.concatenate(
        [
            lax.dynamic_slice_in_dim(key_rows, kv_first * HD, kv_heads * HD, 1),
            lax.dynamic_slice_in_dim(val_rows, kv_first * HD, kv_heads * HD, 1),
        ],
        1,
    )
    earlier = [own_suffix] + [
        shifted_back(own_suffix, "seq", distance) for distance in range(1, back_blocks + 1)
    ]
    suffix_window = jnp.stack(earlier, 0)
    query_full = jnp.dot(normed, w_query, preferred_element_type=jnp.float32)
    queries = (
        rotate(query_full, P_SIZE + offset, query_heads)
        .astype(jnp.bfloat16)
        .reshape(token_rows, kv_heads, repeat_count, HD)
    )
    running = (
        jnp.full((kv_heads, repeat_count, token_rows), -1e30, jnp.float32),
        jnp.zeros((kv_heads, repeat_count, token_rows), jnp.float32),
        jnp.zeros((kv_heads, repeat_count, token_rows, HD), jnp.float32),
    )
    sources_per_chunk = max(1, PREFIX_CHUNK // prefix_rows)
    chunks_per_group = seq_devices // sources_per_chunk
    first_group = group_of[0]
    last_group = group_of[token_rows - 1]

    def prefix_step(chunk, state_now):
        group = chunk // chunks_per_group
        part = chunk % chunks_per_group
        block = lax.dynamic_slice(
            all_prefix,
            (part * sources_per_chunk, group, 0, 0),
            (sources_per_chunk, 1, prefix_rows, block_width),
        ).reshape(sources_per_chunk * prefix_rows, block_width)
        allowed = jnp.broadcast_to(
            (group_of == group)[:, None], (token_rows, sources_per_chunk * prefix_rows)
        )
        return attend(state_now, queries, block, allowed)

    running = lax.fori_loop(
        first_group * chunks_per_group, (last_group + 1) * chunks_per_group, prefix_step, running
    )
    first_block = starts[request[0]] // token_rows
    back_needed = jnp.minimum(seq_index - first_block, back_blocks)

    def suffix_step(distance, state_now):
        source_dev = seq_index - distance
        key_place = source_dev * token_rows + jnp.arange(token_rows, dtype=jnp.int32)
        key_request = jnp.sum((key_place[:, None] >= request_end[None, :]).astype(jnp.int32), 1)
        allowed = (
            (request[:, None] == key_request[None, :])
            & (key_place[None, :] <= position[:, None])
            & (source_dev >= 0)
        )
        block = lax.dynamic_index_in_dim(suffix_window, distance, 0, keepdims=False)
        return attend(state_now, queries, block, allowed)

    running = lax.fori_loop(0, back_needed + 1, suffix_step, running)
    final_max, final_sum, numerator = running
    context = numerator / final_sum[..., None]
    context = (
        jnp.transpose(context, (2, 0, 1, 3))
        .reshape(token_rows, query_heads * HD)
        .astype(jnp.bfloat16)
    )
    mixture = jnp.dot(context, w_out, preferred_element_type=jnp.float32)
    mixture = lax.psum_scatter(
        mixture.astype(jnp.bfloat16), "mp", scatter_dimension=1, tiled=True
    ).astype(jnp.float32)
    own_columns = lax.dynamic_slice_in_dim(activations, mp_index * part_width, part_width, 1)
    hidden = (own_columns + mixture).astype(jnp.bfloat16)
    local_last = request_end - 1 - seq_index * token_rows
    onehot = (local_last[:, None] == jnp.arange(token_rows, dtype=jnp.int32)[None, :]).astype(
        jnp.bfloat16
    )
    last_part = jnp.dot(onehot, hidden, preferred_element_type=jnp.float32).astype(jnp.bfloat16)
    last_part = lax.psum(last_part, "seq")
    last_rows = lax.all_gather(last_part, "mp", axis=1, tiled=True).astype(jnp.float32)
    inv_rms = lax.rsqrt(jnp.mean(last_rows * last_rows, -1, keepdims=True) + epsilon)
    last_normed = (last_rows * final_gain.astype(jnp.float32) * inv_rms).astype(jnp.bfloat16)
    logits = jnp.dot(last_normed, w_head, preferred_element_type=jnp.float32)
    greatest = lax.pmax(jnp.max(logits, -1), ("seq", "mp"))
    return (hidden, suffix_cache, last_normed, greatest)


def solution(mesh):
    return jax.shard_map(
        per_device,
        mesh=mesh,
        in_specs=(
            P("seq", None),
            P(),
            P(None, "seq", None),
            P(),
            P(None, "mp"),
            P(),
            P("mp", None),
            P(),
            P(None, ("seq", "mp")),
        ),
        out_specs=(P("seq", "mp"), P("seq", None), P(), P()),
        check_vma=False,
    )
```

profile of v0, /device:TPU:0, one launch (start us, length us, event | category | flops | bytes accessed | tf_op | source)
XLA Modules:
  0.0 349.4 jit_solution(14837220267693971893)
XLA Ops:
  11.6 2.0 fusion.24
  19.5 3.0 collective-permute-start
  22.5 4.4 %collective-permute-start.1 = (bf16[256,256]{1,0:T(8,128)(2,1)}, bf16[256,256]{1,0:T(8,128)(2,1)}, u32[]{:S(2)}, u32[]{:S(2)}) collective-permute-start(bf16[256,256]{1,0:T(8,128)(2,1)} %pad_maximum_fusion.4), channel_id=1, source_target_pairs={{0,4},{2,6},{4,8},{6,10},{8,12},{10,14},{12,16},{14,18},{16,20},{1... | collective-permute-start | bytes 393224 | tf_op jit(solution)/shard_map/ppermute | solution.py:57
  26.9 4.4 %collective-permute-start.2 = (bf16[256,256]{1,0:T(8,128)(2,1)}, bf16[256,256]{1,0:T(8,128)(2,1)}, u32[]{:S(2)}, u32[]{:S(2)}) collective-permute-start(bf16[256,256]{1,0:T(8,128)(2,1)} %pad_maximum_fusion.4), channel_id=1, source_target_pairs={{0,6},{2,8},{4,10},{6,12},{8,14},{10,16},{12,18},{14,20},{16,22},{... | collective-permute-start | bytes 393224 | tf_op jit(solution)/shard_map/ppermute | solution.py:57
  31.4 3.5 collective-permute-start.3
  35.5 4.0 %fusion.25 = f32[256,1024]{0,1:T(8,128)S(1)} fusion(bf16[2048,1024]{1,0:T(8,128)(2,1)} %param.17, f32[2048]{0:T(1024)S(1)} %convert_element_type.75, f32[256]{0:T(256)} %copy-done.17, bf16[256,2048]{1,0:T(8,128)(2,1)S(1)} %copy-done.4), kind=kOutput, calls=%fused_computation.46 | convolution fusion | flops 1075838976 | bytes 6300672 | tf_op jit(solution)/shard_map/dot_general | solution.py:115
  51.9 1.6 bitcast_dynamic-update-slice_fusion
  53.5 13.9 %all-gather.3.cloned.1.call-done = bf16[64,128,256]{2,1,0:T(8,128)(2,1)} async-done(((bf16[4,128,256]{2,1,0:T(8,128)(2,1)}), bf16[64,128,256]{2,1,0:T(8,128)(2,1)}) %all-gather.3.cloned.1.call-update) | async-done | bytes 4194320 | tf_op jit(solution)/shard_map/all_gather | solution.py:86
  68.6 49.2 %while.31 = (s32[]{:T(128)}, f32[2,8,256]{2,1,0:T(8,128)S(1)}, f32[2,8,256]{2,1,0:T(8,128)S(1)}, f32[2,8,256,64]{2,3,1,0:T(8,128)}, s32[]{:T(128)}, /*index=5*/s...) while((s32[]{:T(128)}, f32[2,8,256]{2,1,0:T(8,128)S(1)}, ...), condition=%wide.region_7.8_spmd, body=%wide.region_4.7_spmd.sunk | while | flops 560472320 | bytes 63441352 | solution.py:144
  71.0 1.7 fusion.66
  74.4 6.5 %fusion.67 = f32[2,8,256,64]{2,3,1,0:T(8,128)} fusion(bf16[512,2,64,1]{0,2,3,1:T(8,128)(2,1)S(1)} %bitcast.123, f32[2,512,256,8]{2,1,3,0:T(8,128)} %copy-done.1, f32[2,8,256]{2,1,0:T(8,128)S(1)} %max.14, pred[256]{0:T(512)(128)(4,1)S(1)} %broadcast_compare_fusion.2, f32[2,8,256,64]{2,3,1,0:T(8,128)} %get-tuple-element.501, ...), kind=kOutput, calls=%fused_computation.9.clone.1 | convolution fusion | flops 277348352 | bytes 10649856 | tf_op jit(solution)/shard_map/while/body/grqn,ngd->grqd/dot_general | solution.py:48
  83.3 1.7 fusion.66
  86.7 6.5 %fusion.67 = f32[2,8,256,64]{2,3,1,0:T(8,128)} fusion(bf16[512,2,64,1]{0,2,3,1:T(8,128)(2,1)S(1)} %bitcast.123, f32[2,512,256,8]{2,1,3,0:T(8,128)} %copy-done.1, f32[2,8,256]{2,1,0:T(8,128)S(1)} %max.14, pred[256]{0:T(512)(128)(4,1)S(1)} %broadcast_compare_fusion.2, f32[2,8,256,64]{2,3,1,0:T(8,128)} %get-tuple-element.501, ...), kind=kOutput, calls=%fused_computation.9.clone.1 | convolution fusion | flops 277348352 | bytes 10649856 | tf_op jit(solution)/shard_map/while/body/grqn,ngd->grqd/dot_general | solution.py:48
  95.6 1.7 fusion.66
  99.0 6.5 %fusion.67 = f32[2,8,256,64]{2,3,1,0:T(8,128)} fusion(bf16[512,2,64,1]{0,2,3,1:T(8,128)(2,1)S(1)} %bitcast.123, f32[2,512,256,8]{2,1,3,0:T(8,128)} %copy-done.1, f32[2,8,256]{2,1,0:T(8,128)S(1)} %max.14, pred[256]{0:T(512)(128)(4,1)S(1)} %broadcast_compare_fusion.2, f32[2,8,256,64]{2,3,1,0:T(8,128)} %get-tuple-element.501, ...), kind=kOutput, calls=%fused_computation.9.clone.1 | convolution fusion | flops 277348352 | bytes 10649856 | tf_op jit(solution)/shard_map/while/body/grqn,ngd->grqd/dot_general | solution.py:48
  108.0 1.7 fusion.66
  111.3 6.5 %fusion.67 = f32[2,8,256,64]{2,3,1,0:T(8,128)} fusion(bf16[512,2,64,1]{0,2,3,1:T(8,128)(2,1)S(1)} %bitcast.123, f32[2,512,256,8]{2,1,3,0:T(8,128)} %copy-done.1, f32[2,8,256]{2,1,0:T(8,128)S(1)} %max.14, pred[256]{0:T(512)(128)(4,1)S(1)} %broadcast_compare_fusion.2, f32[2,8,256,64]{2,3,1,0:T(8,128)} %get-tuple-element.501, ...), kind=kOutput, calls=%fused_computation.9.clone.1 | convolution fusion | flops 277348352 | bytes 10649856 | tf_op jit(solution)/shard_map/while/body/grqn,ngd->grqd/dot_general | solution.py:48
  117.8 5.3 %while.32 = (s32[]{:T(128)}, f32[2,8,256]{2,1,0:T(8,128)S(1)}, f32[2,8,256]{2,1,0:T(8,128)S(1)}, f32[2,8,256,64]{2,3,1,0:T(8,128)}, s32[]{:T(128)}, /*index=5*/s...) while((s32[]{:T(128)}, f32[2,8,256]{2,1,0:T(8,128)S(1)}, ...), condition=%wide.region_12.13_spmd.clone, body=%wide.region_8.12_spmd.clone.sunk | while | flops 280789248 | bytes 25043356 | solution.py:162
  124.4 4.6 %convolution_convert_fusion = bf16[256,2048]{1,0:T(8,128)(2,1)} fusion(bf16[256,1024]{0,1:T(8,128)(2,1)S(1)} %bitcast.126, bf16[1024,2048]{1,0:T(8,128)(2,1)} %param.19), kind=kOutput, calls=%fused_computation.33 | convolution fusion | flops 1074266112 | bytes 5767168 | tf_op jit(solution)/shard_map/dot_general | solution.py:170
  130.6 71.8 %reduce-scatter.2.cloned.1.call-done = bf16[256,1024]{1,0:T(8,128)(2,1)} async-done(((bf16[256,2048]{1,0:T(8,128)(2,1)}), bf16[256,1024]{1,0:T(8,128)(2,1)}) %reduce-scatter.2.cloned.1.call-update) | async-done | bytes 524304 | tf_op jit(solution)/shard_map/reduce_scatter | solution.py:171
  204.9 86.4 %all-reduce.2.cloned.1.call-done = bf16[32,1024]{1,0:T(8,128)(2,1)} async-done(((bf16[32,1024]{1,0:T(8,128)(2,1)}), bf16[32,1024]{1,0:T(8,128)(2,1)}) %all-reduce.2.cloned.1.call-update) | async-done | bytes 65552 | tf_op jit(solution)/shard_map/psum | solution.py:181
  291.4 5.2 %all_gather.11 = bf16[32,2048]{1,0:T(8,128)(2,1)S(1)} all-gather(bf16[32,1024]{1,0:T(8,128)(2,1)} %all-reduce.2.cloned.1.call-done), channel_id=1, replica_groups=mesh['seq'=16,'mp'=2] {'mp'}, dimensions={1}, use_global_device_ids=true | all-gather | bytes 196608 | tf_op jit(solution)/shard_map/all_gather | solution.py:182
  296.8 3.6 %convolution_reduce_fusion = f32[32]{0:T(128)S(1)} fusion(bf16[32,2048]{1,0:T(8,128)(2,1)S(1)} %fusion.27, bf16[2048,1000]{0,1:T(8,128)(2,1)} %param.21), kind=kOutput, calls=%fused_computation.37 | convolution fusion | flops 131103968 | bytes 4227200 | tf_op jit(solution)/shard_map/dot_general | solution.py:185
  301.1 41.7 %pmax.7 = f32[32]{0:T(128)} all-reduce(f32[32]{0:T(128)S(1)} %convolution_reduce_fusion), channel_id=1, replica_groups=mesh['seq'=16,'mp'=2] {'seq','mp'}, use_global_device_ids=true, to_apply=%region_17.18 | all-reduce | flops 32 | bytes 256 | tf_op jit(solution)/shard_map/pmax | solution.py:186
  (145 shorter events, 46.5 us)
Async XLA Ops:
  7.2 4.5 %copy-start = (bf16[2048,512]{1,0:T(8,128)(2,1)S(1)}, bf16[2048,512]{1,0:T(8,128)(2,1)}, u32[]{:S(2)}) copy-start(bf16[2048,512]{1,0:T(8,128)(2,1)} %param.18) | copy-start | bytes 6291460
  7.2 7.3 %copy-start.13 = (s32[32]{0:T(128)S(1)}, s32[32]{0:T(128)}, u32[]{:S(2)}) copy-start(s32[32]{0:T(128)} %param.14) | copy-start | bytes 388
  7.2 60.2 %all-gather.3.cloned.1.call-start = ((), (), s32[]{:S(2)}) async-start(), calls=%async_computation.3 | async-start | bytes 4456448 | tf_op jit(solution)/shard_map/all_gather | solution.py:86
  9.3 193.1 %reduce-scatter.2.cloned.1.call-start = ((), (), s32[]{:S(2)}) async-start(), calls=%async_computation.1 | async-start | bytes 1572864 | tf_op jit(solution)/shard_map/reduce_scatter | solution.py:171
  11.6 23.9 %copy-start.4 = (bf16[256,2048]{1,0:T(8,128)(2,1)S(1)}, bf16[256,2048]{1,0:T(8,128)(2,1)}, u32[]{:S(2)}) copy-start(bf16[256,2048]{1,0:T(8,128)(2,1)} %param.13) | copy-start | bytes 3145732
  11.6 2.9 copy-start.17
  18.7 20.9 %copy-start.9 = (f32[256,32]{0,1:T(8,128)S(1)}, f32[256,32]{0,1:T(8,128)}, u32[]{:S(2)}) copy-start(f32[256,32]{0,1:T(8,128)} %copy-done.8) | copy-start | bytes 98308
  18.7 20.9 %copy-start.11 = (f32[256,32]{0,1:T(8,128)S(1)}, f32[256,32]{0,1:T(8,128)}, u32[]{:S(2)}) copy-start(f32[256,32]{0,1:T(8,128)} %copy-done.10) | copy-start | bytes 98308
  19.5 27.7 %collective-permute-start = (bf16[256,256]{1,0:T(8,128)(2,1)}, bf16[256,256]{1,0:T(8,128)(2,1)}, u32[]{:S(2)}, u32[]{:S(2)}) collective-permute-start(bf16[256,256]{1,0:T(8,128)(2,1)} %pad_maximum_fusion.4), channel_id=1, source_target_pairs={{0,2},{2,4},{4,6},{6,8},{8,10},{10,12},{12,14},{14,16},{16,18},{18... | collective-permute-start | bytes 393224 | tf_op jit(solution)/shard_map/ppermute | solution.py:57
  22.5 26.3 %collective-permute-start.1 = (bf16[256,256]{1,0:T(8,128)(2,1)}, bf16[256,256]{1,0:T(8,128)(2,1)}, u32[]{:S(2)}, u32[]{:S(2)}) collective-permute-start(bf16[256,256]{1,0:T(8,128)(2,1)} %pad_maximum_fusion.4), channel_id=1, source_target_pairs={{0,4},{2,6},{4,8},{6,10},{8,12},{10,14},{12,16},{14,18},{16,20},{1... | collective-permute-start | bytes 393224 | tf_op jit(solution)/shard_map/ppermute | solution.py:57
  26.9 23.4 %collective-permute-start.2 = (bf16[256,256]{1,0:T(8,128)(2,1)}, bf16[256,256]{1,0:T(8,128)(2,1)}, u32[]{:S(2)}, u32[]{:S(2)}) collective-permute-start(bf16[256,256]{1,0:T(8,128)(2,1)} %pad_maximum_fusion.4), channel_id=1, source_target_pairs={{0,6},{2,8},{4,10},{6,12},{8,14},{10,16},{12,18},{14,20},{16,22},{... | collective-permute-start | bytes 393224 | tf_op jit(solution)/shard_map/ppermute | solution.py:57
  31.4 20.5 %collective-permute-start.3 = (bf16[256,256]{1,0:T(8,128)(2,1)}, bf16[256,256]{1,0:T(8,128)(2,1)}, u32[]{:S(2)}, u32[]{:S(2)}) collective-permute-start(bf16[256,256]{1,0:T(8,128)(2,1)} %pad_maximum_fusion.4), channel_id=1, source_target_pairs={{0,8},{2,10},{4,12},{6,14},{8,16},{10,18},{12,20},{14,22},{16,24},... | collective-permute-start | bytes 393224 | tf_op jit(solution)/shard_map/ppermute | solution.py:57
  35.5 7.2 %copy-start.15 = (s32[32]{0:T(128)S(1)}, s32[32]{0:T(128)}, u32[]{:S(2)}) copy-start(s32[32]{0:T(128)} %copy-done.14) | copy-start | bytes 388
  71.0 3.2 copy-start.1
  83.3 3.2 copy-start.1
  95.6 3.2 copy-start.1
  107.9 3.2 copy-start.1
  119.1 1.7 copy-start.2
  124.4 4.6 %copy-start.5 = (bf16[256,2048]{1,0:T(8,128)(2,1)S(1)}, bf16[256,2048]{1,0:T(8,128)(2,1)}, u32[]{:S(2)}) copy-start(bf16[256,2048]{1,0:T(8,128)(2,1)} %param.13) | copy-start | bytes 3145732
  129.0 75.0 %copy-start.16 = (s32[32]{0:T(128)S(1)}, s32[32]{0:T(128)}, u32[]{:S(2)}) copy-start(s32[32]{0:T(128)} %get-tuple-element.333) | copy-start | bytes 388
  129.0 75.9 %copy-start.12 = (bf16[2048]{0:T(1024)(128)(2,1)S(1)}, bf16[2048]{0:T(1024)(128)(2,1)}, u32[]{:S(2)}) copy-start(bf16[2048]{0:T(1024)(128)(2,1)} %param.20) | copy-start | bytes 12292
  129.0 162.4 %all-reduce.2.cloned.1.call-start = ((), (), s32[]{:S(2)}) async-start(), calls=%async_computation.2 | async-start | bytes 131072 | tf_op jit(solution)/shard_map/psum | solution.py:181
  204.0 138.9 %copy-start.6 = (bf16[256,1024]{1,0:T(8,128)(2,1)}, bf16[256,1024]{1,0:T(8,128)(2,1)S(1)}, u32[]{:S(2)}) copy-start(bf16[256,1024]{1,0:T(8,128)(2,1)S(1)} %add_convert_fusion) | copy-start | bytes 1572868
  296.8 46.1 %copy-start.7 = (bf16[32,2048]{1,0:T(8,128)(2,1)}, bf16[32,2048]{1,0:T(8,128)(2,1)S(1)}, u32[]{:S(2)}) copy-start(bf16[32,2048]{1,0:T(8,128)(2,1)S(1)} %fusion.27) | copy-start | bytes 393220
  (4 other events, 2.9 us)
Sparse Core Ops, SparseCore 0:
  10.8 56.5 all-gather.2
  129.1 73.2 reduce-scatter.1
  206.9 84.4 all-reduce.1
where the time goes:
time: 350 us; the launch traced here: 349 us
  waiting for transfers between devices  172 us (49%)
  matrix products  48.3 us (14%)
  blocking collectives  46.9 us (13%)
  local copies, waits for them, and re-layouts  26.9 us (8%)
  between operations  19.7 us (6%)
  other arithmetic  19.6 us (6%)
  starting transfers between devices  15.5 us (4%)
    psum x1, waiting for transfers between devices, per_device(): last_part = lax.psum(last_part, 'seq')  86.4 us
    reduce_scatter x1, waiting for transfers between devices, per_device(): lax.psum_scatter(mixture.astype(jnp.bfloat16), 'mp', scatter_dimension=1,...  71.8 us
    pmax x1, blocking collectives, per_device(): greatest = lax.pmax(jnp.max(logits, -1), ('seq', 'mp'))  41.7 us
    dot_general x5, matrix products, attend(): jnp.einsum('grqn,ngd->grqd', weights.astype(jnp.bfloat16), val_rows, pref...  27.2 us
    ppermute x4, starting transfers between devices, shifted_back(): return lax.ppermute(block, axis, route)  15.3 us
    all_gather x1, waiting for transfers between devices, per_device(): all_prefix = lax.all_gather(own_prefix, 'seq', axis=0)  13.9 us
    while x25, local copies, waits for them, and re-layouts  8.14 us
    reduce_sum x5, other arithmetic, attend(): new_sum = old_sum * factor + jnp.sum(weights, -1)  7.48 us
  transfers between devices with their start and end apart: 7, of which 3 were waited for; matrix products, arithmetic and copies ran while one was open for 7% of the time, Pallas kernels for 0%

commit v1 on v0

--- a/solution.py
+++ b/solution.py
@@ -3,6 +3,7 @@
 import jax.numpy as jnp
 from jax import lax
 from jax.sharding import PartitionSpec as P
+from jax.lax import all_gather
 
 QH = 32
 KVH = 4
@@ -178,7 +179,7 @@
         jnp.bfloat16
     )
     last_part = jnp.dot(onehot, hidden, preferred_element_type=jnp.float32).astype(jnp.bfloat16)
-    last_part = lax.psum(last_part, "seq")
+    last_part = jnp.sum(all_gather(last_part, axis_name="seq"), 0)
     last_rows = lax.all_gather(last_part, "mp", axis=1, tiled=True).astype(jnp.float32)
     inv_rms = lax.rsqrt(jnp.mean(last_rows * last_rows, -1, keepdims=True) + epsilon)
     last_normed = (last_rows * final_gain.astype(jnp.float32) * inv_rms).astype(jnp.bfloat16)

time: 350 us -> 301 us (0.86)
  waiting for transfers between devices: 172 us -> 124 us
    psum x1 -> x0, waiting for transfers between devices: 86.4 us -> none  [per_device(): last_part = lax.psum(last_part, 'seq')]
    all_gather x0 -> x1, waiting for transfers between devices: none -> 38.5 us  [per_device(): last_part = jnp.sum(all_gather(last_part, axis_name='seq'), 0)]
  transfers between devices with their start and end apart: 7 -> 7, of which waited for: 3 -> 3; matrix products, arithmetic and copies ran while one was open for 7% -> 8% of each run, Pallas kernels for 0% -> 0%
where the time goes in v1:
time: 301 us; the launch traced here: 300 us
  waiting for transfers between devices  124 us (41%)
  matrix products  48.3 us (16%)
  blocking collectives  43.7 us (15%)
  local copies, waits for them, and re-layouts  26.9 us (9%)
  other arithmetic  21 us (7%)
  between operations  19.7 us (7%)
  starting transfers between devices  15.5 us (5%)
    reduce_scatter x1, waiting for transfers between devices, per_device(): lax.psum_scatter(mixture.astype(jnp.bfloat16), 'mp', scatter_dimension=1,...  71.8 us
    pmax x1, blocking collectives, per_device(): greatest = lax.pmax(jnp.max(logits, -1), ('seq', 'mp'))  38.8 us
    all_gather x1, waiting for transfers between devices, per_device(): last_part = jnp.sum(all_gather(last_part, axis_name='seq'), 0)  38.5 us
    dot_general x5, matrix products, attend(): jnp.einsum('grqn,ngd->grqd', weights.astype(jnp.bfloat16), val_rows, pref...  27.2 us
    ppermute x4, starting transfers between devices, shifted_back(): return lax.ppermute(block, axis, route)  15.3 us
    all_gather x1, waiting for transfers between devices, per_device(): all_prefix = lax.all_gather(own_prefix, 'seq', axis=0)  13.9 us
    while x25, local copies, waits for them, and re-layouts  8.14 us
    reduce_sum x5, other arithmetic, attend(): new_sum = old_sum * factor + jnp.sum(weights, -1)  7.48 us
  transfers between devices with their start and end apart: 7, of which 3 were waited for; matrix products, arithmetic and copies ran while one was open for 8% of the time, Pallas kernels for 0%

profile of v1, /device:TPU:0, one launch (start us, length us, event | category | flops | bytes accessed | tf_op | source)
XLA Modules:
  0.0 299.7 jit_solution(13687479178398181889)
XLA Ops:
  11.6 2.0 fusion.24
  19.5 3.0 %collective-permute-start = (bf16[256,256]{1,0:T(8,128)(2,1)}, bf16[256,256]{1,0:T(8,128)(2,1)}, u32[]{:S(2)}, u32[]{:S(2)}) collective-permute-start(bf16[256,256]{1,0:T(8,128)(2,1)} %pad_maximum_fusion.4), channel_id=1, source_target_pairs={{0,2},{2,4},{4,6},{6,8},{8,10},{10,12},{12,14},{14,16},{16,18},{18... | collective-permute-start | bytes 393224 | tf_op jit(solution)/shard_map/ppermute | solution.py:58
  22.5 4.4 %collective-permute-start.1 = (bf16[256,256]{1,0:T(8,128)(2,1)}, bf16[256,256]{1,0:T(8,128)(2,1)}, u32[]{:S(2)}, u32[]{:S(2)}) collective-permute-start(bf16[256,256]{1,0:T(8,128)(2,1)} %pad_maximum_fusion.4), channel_id=1, source_target_pairs={{0,4},{2,6},{4,8},{6,10},{8,12},{10,14},{12,16},{14,18},{16,20},{1... | collective-permute-start | bytes 393224 | tf_op jit(solution)/shard_map/ppermute | solution.py:58
  26.9 4.4 %collective-permute-start.2 = (bf16[256,256]{1,0:T(8,128)(2,1)}, bf16[256,256]{1,0:T(8,128)(2,1)}, u32[]{:S(2)}, u32[]{:S(2)}) collective-permute-start(bf16[256,256]{1,0:T(8,128)(2,1)} %pad_maximum_fusion.4), channel_id=1, source_target_pairs={{0,6},{2,8},{4,10},{6,12},{8,14},{10,16},{12,18},{14,20},{16,22},{... | collective-permute-start | bytes 393224 | tf_op jit(solution)/shard_map/ppermute | solution.py:58
  31.4 3.5 %collective-permute-start.3 = (bf16[256,256]{1,0:T(8,128)(2,1)}, bf16[256,256]{1,0:T(8,128)(2,1)}, u32[]{:S(2)}, u32[]{:S(2)}) collective-permute-start(bf16[256,256]{1,0:T(8,128)(2,1)} %pad_maximum_fusion.4), channel_id=1, source_target_pairs={{0,8},{2,10},{4,12},{6,14},{8,16},{10,18},{12,20},{14,22},{16,24},... | collective-permute-start | bytes 393224 | tf_op jit(solution)/shard_map/ppermute | solution.py:58
  35.5 4.0 %fusion.25 = f32[256,1024]{0,1:T(8,128)S(1)} fusion(bf16[2048,1024]{1,0:T(8,128)(2,1)} %param.17, f32[2048]{0:T(1024)S(1)} %convert_element_type.77, f32[256]{0:T(256)} %copy-done.17, bf16[256,2048]{1,0:T(8,128)(2,1)S(1)} %copy-done.4), kind=kOutput, calls=%fused_computation.46 | convolution fusion | flops 1075838976 | bytes 6300672 | tf_op jit(solution)/shard_map/dot_general | solution.py:116
  51.9 1.6 bitcast_dynamic-update-slice_fusion
  53.5 13.9 %all-gather.5.cloned.1.call-done = bf16[64,128,256]{2,1,0:T(8,128)(2,1)} async-done(((bf16[4,128,256]{2,1,0:T(8,128)(2,1)}), bf16[64,128,256]{2,1,0:T(8,128)(2,1)}) %all-gather.5.cloned.1.call-update) | async-done | bytes 4194320 | tf_op jit(solution)/shard_map/all_gather | solution.py:87
  68.6 49.2 %while.31 = (s32[]{:T(128)}, f32[2,8,256]{2,1,0:T(8,128)S(1)}, f32[2,8,256]{2,1,0:T(8,128)S(1)}, f32[2,8,256,64]{2,3,1,0:T(8,128)}, s32[]{:T(128)}, /*index=5*/s...) while((s32[]{:T(128)}, f32[2,8,256]{2,1,0:T(8,128)S(1)}, ...), condition=%wide.region_7.8_spmd, body=%wide.region_4.7_spmd.sunk | while | flops 560472320 | bytes 63441352 | solution.py:145
  71.0 1.7 fusion.66
  74.4 6.5 %fusion.67 = f32[2,8,256,64]{2,3,1,0:T(8,128)} fusion(bf16[512,2,64,1]{0,2,3,1:T(8,128)(2,1)S(1)} %bitcast.124, f32[2,512,256,8]{2,1,3,0:T(8,128)} %copy-done.1, f32[2,8,256]{2,1,0:T(8,128)S(1)} %max.14, pred[256]{0:T(512)(128)(4,1)S(1)} %broadcast_compare_fusion.2, f32[2,8,256,64]{2,3,1,0:T(8,128)} %get-tuple-element.501, ...), kind=kOutput, calls=%fused_computation.9.clone.1 | convolution fusion | flops 277348352 | bytes 10649856 | tf_op jit(solution)/shard_map/while/body/grqn,ngd->grqd/dot_general | solution.py:49
  83.3 1.7 fusion.66
  86.7 6.5 %fusion.67 = f32[2,8,256,64]{2,3,1,0:T(8,128)} fusion(bf16[512,2,64,1]{0,2,3,1:T(8,128)(2,1)S(1)} %bitcast.124, f32[2,512,256,8]{2,1,3,0:T(8,128)} %copy-done.1, f32[2,8,256]{2,1,0:T(8,128)S(1)} %max.14, pred[256]{0:T(512)(128)(4,1)S(1)} %broadcast_compare_fusion.2, f32[2,8,256,64]{2,3,1,0:T(8,128)} %get-tuple-element.501, ...), kind=kOutput, calls=%fused_computation.9.clone.1 | convolution fusion | flops 277348352 | bytes 10649856 | tf_op jit(solution)/shard_map/while/body/grqn,ngd->grqd/dot_general | solution.py:49
  95.6 1.7 fusion.66
  99.0 6.5 %fusion.67 = f32[2,8,256,64]{2,3,1,0:T(8,128)} fusion(bf16[512,2,64,1]{0,2,3,1:T(8,128)(2,1)S(1)} %bitcast.124, f32[2,512,256,8]{2,1,3,0:T(8,128)} %copy-done.1, f32[2,8,256]{2,1,0:T(8,128)S(1)} %max.14, pred[256]{0:T(512)(128)(4,1)S(1)} %broadcast_compare_fusion.2, f32[2,8,256,64]{2,3,1,0:T(8,128)} %get-tuple-element.501, ...), kind=kOutput, calls=%fused_computation.9.clone.1 | convolution fusion | flops 277348352 | bytes 10649856 | tf_op jit(solution)/shard_map/while/body/grqn,ngd->grqd/dot_general | solution.py:49
  108.0 1.7 fusion.66
  111.3 6.5 %fusion.67 = f32[2,8,256,64]{2,3,1,0:T(8,128)} fusion(bf16[512,2,64,1]{0,2,3,1:T(8,128)(2,1)S(1)} %bitcast.124, f32[2,512,256,8]{2,1,3,0:T(8,128)} %copy-done.1, f32[2,8,256]{2,1,0:T(8,128)S(1)} %max.14, pred[256]{0:T(512)(128)(4,1)S(1)} %broadcast_compare_fusion.2, f32[2,8,256,64]{2,3,1,0:T(8,128)} %get-tuple-element.501, ...), kind=kOutput, calls=%fused_computation.9.clone.1 | convolution fusion | flops 277348352 | bytes 10649856 | tf_op jit(solution)/shard_map/while/body/grqn,ngd->grqd/dot_general | solution.py:49
  117.8 5.3 %while.32 = (s32[]{:T(128)}, f32[2,8,256]{2,1,0:T(8,128)S(1)}, f32[2,8,256]{2,1,0:T(8,128)S(1)}, f32[2,8,256,64]{2,3,1,0:T(8,128)}, s32[]{:T(128)}, /*index=5*/s...) while((s32[]{:T(128)}, f32[2,8,256]{2,1,0:T(8,128)S(1)}, ...), condition=%wide.region_12.13_spmd.clone, body=%wide.region_8.12_spmd.clone.sunk | while | flops 280789248 | bytes 25043356 | solution.py:163
  124.4 4.6 %convolution_convert_fusion = bf16[256,2048]{1,0:T(8,128)(2,1)} fusion(bf16[256,1024]{0,1:T(8,128)(2,1)S(1)} %bitcast.128, bf16[1024,2048]{1,0:T(8,128)(2,1)} %param.19), kind=kOutput, calls=%fused_computation.33 | convolution fusion | flops 1074266112 | bytes 5767168 | tf_op jit(solution)/shard_map/dot_general | solution.py:171
  130.6 71.8 %reduce-scatter.2.cloned.1.call-done = bf16[256,1024]{1,0:T(8,128)(2,1)} async-done(((bf16[256,2048]{1,0:T(8,128)(2,1)}), bf16[256,1024]{1,0:T(8,128)(2,1)}) %reduce-scatter.2.cloned.1.call-update) | async-done | bytes 524304 | tf_op jit(solution)/shard_map/reduce_scatter | solution.py:172
  204.9 38.5 %all-gather.7.cloned.1.call-done = bf16[512,1024]{1,0:T(8,128)(2,1)} async-done(((bf16[32,1024]{1,0:T(8,128)(2,1)}), bf16[512,1024]{1,0:T(8,128)(2,1)}) %all-gather.7.cloned.1.call-update) | async-done | bytes 1048592 | tf_op jit(solution)/shard_map/all_gather | solution.py:182
  244.8 4.9 %all_gather.19 = bf16[32,2048]{1,0:T(8,128)(2,1)S(1)} all-gather(bf16[32,1024]{1,0:T(8,128)(2,1)S(1)} %reduce_sum.81), channel_id=1, replica_groups=mesh['seq'=16,'mp'=2] {'mp'}, dimensions={1}, use_global_device_ids=true | all-gather | bytes 196608 | tf_op jit(solution)/shard_map/all_gather | solution.py:183
  250.0 3.6 %convolution_reduce_fusion = f32[32]{0:T(128)S(1)} fusion(bf16[32,2048]{1,0:T(8,128)(2,1)S(1)} %fusion.27, bf16[2048,1000]{0,1:T(8,128)(2,1)} %param.21), kind=kOutput, calls=%fused_computation.37 | convolution fusion | flops 131103968 | bytes 4227200 | tf_op jit(solution)/shard_map/dot_general | solution.py:186
  254.3 38.8 %pmax.7 = f32[32]{0:T(128)} all-reduce(f32[32]{0:T(128)S(1)} %convolution_reduce_fusion), channel_id=1, replica_groups=mesh['seq'=16,'mp'=2] {'seq','mp'}, use_global_device_ids=true, to_apply=%region_17.18 | all-reduce | flops 32 | bytes 256 | tf_op jit(solution)/shard_map/pmax | solution.py:187
  (146 shorter events, 47.9 us)
Async XLA Ops:
  7.2 4.5 %copy-start = (bf16[2048,512]{1,0:T(8,128)(2,1)S(1)}, bf16[2048,512]{1,0:T(8,128)(2,1)}, u32[]{:S(2)}) copy-start(bf16[2048,512]{1,0:T(8,128)(2,1)} %param.18) | copy-start | bytes 6291460
  7.2 7.3 %copy-start.13 = (s32[32]{0:T(128)S(1)}, s32[32]{0:T(128)}, u32[]{:S(2)}) copy-start(s32[32]{0:T(128)} %param.14) | copy-start | bytes 388
  7.2 60.2 %all-gather.5.cloned.1.call-start = ((), (), s32[]{:S(2)}) async-start(), calls=%async_computation.2 | async-start | bytes 4456448 | tf_op jit(solution)/shard_map/all_gather | solution.py:87
  9.3 193.1 %reduce-scatter.2.cloned.1.call-start = ((), (), s32[]{:S(2)}) async-start(), calls=%async_computation.1 | async-start | bytes 1572864 | tf_op jit(solution)/shard_map/reduce_scatter | solution.py:172
  11.6 23.9 %copy-start.4 = (bf16[256,2048]{1,0:T(8,128)(2,1)S(1)}, bf16[256,2048]{1,0:T(8,128)(2,1)}, u32[]{:S(2)}) copy-start(bf16[256,2048]{1,0:T(8,128)(2,1)} %param.13) | copy-start | bytes 3145732
  11.6 2.9 copy-start.17
  18.7 20.9 %copy-start.9 = (f32[256,32]{0,1:T(8,128)S(1)}, f32[256,32]{0,1:T(8,128)}, u32[]{:S(2)}) copy-start(f32[256,32]{0,1:T(8,128)} %copy-done.8) | copy-start | bytes 98308
  18.7 20.9 %copy-start.11 = (f32[256,32]{0,1:T(8,128)S(1)}, f32[256,32]{0,1:T(8,128)}, u32[]{:S(2)}) copy-start(f32[256,32]{0,1:T(8,128)} %copy-done.10) | copy-start | bytes 98308
  19.5 27.7 %collective-permute-start = (bf16[256,256]{1,0:T(8,128)(2,1)}, bf16[256,256]{1,0:T(8,128)(2,1)}, u32[]{:S(2)}, u32[]{:S(2)}) collective-permute-start(bf16[256,256]{1,0:T(8,128)(2,1)} %pad_maximum_fusion.4), channel_id=1, source_target_pairs={{0,2},{2,4},{4,6},{6,8},{8,10},{10,12},{12,14},{14,16},{16,18},{18... | collective-permute-start | bytes 393224 | tf_op jit(solution)/shard_map/ppermute | solution.py:58
  22.5 26.3 %collective-permute-start.1 = (bf16[256,256]{1,0:T(8,128)(2,1)}, bf16[256,256]{1,0:T(8,128)(2,1)}, u32[]{:S(2)}, u32[]{:S(2)}) collective-permute-start(bf16[256,256]{1,0:T(8,128)(2,1)} %pad_maximum_fusion.4), channel_id=1, source_target_pairs={{0,4},{2,6},{4,8},{6,10},{8,12},{10,14},{12,16},{14,18},{16,20},{1... | collective-permute-start | bytes 393224 | tf_op jit(solution)/shard_map/ppermute | solution.py:58
  26.9 23.4 %collective-permute-start.2 = (bf16[256,256]{1,0:T(8,128)(2,1)}, bf16[256,256]{1,0:T(8,128)(2,1)}, u32[]{:S(2)}, u32[]{:S(2)}) collective-permute-start(bf16[256,256]{1,0:T(8,128)(2,1)} %pad_maximum_fusion.4), channel_id=1, source_target_pairs={{0,6},{2,8},{4,10},{6,12},{8,14},{10,16},{12,18},{14,20},{16,22},{... | collective-permute-start | bytes 393224 | tf_op jit(solution)/shard_map/ppermute | solution.py:58
  31.4 20.5 %collective-permute-start.3 = (bf16[256,256]{1,0:T(8,128)(2,1)}, bf16[256,256]{1,0:T(8,128)(2,1)}, u32[]{:S(2)}, u32[]{:S(2)}) collective-permute-start(bf16[256,256]{1,0:T(8,128)(2,1)} %pad_maximum_fusion.4), channel_id=1, source_target_pairs={{0,8},{2,10},{4,12},{6,14},{8,16},{10,18},{12,20},{14,22},{16,24},... | collective-permute-start | bytes 393224 | tf_op jit(solution)/shard_map/ppermute | solution.py:58
  35.5 7.2 %copy-start.15 = (s32[32]{0:T(128)S(1)}, s32[32]{0:T(128)}, u32[]{:S(2)}) copy-start(s32[32]{0:T(128)} %copy-done.14) | copy-start | bytes 388
  71.0 3.2 %copy-start.1 = (f32[2,512,256,8]{2,1,3,0:T(8,128)}, f32[2,512,256,8]{2,1,3,0:T(8,128)S(1)}, u32[]{:S(2)}) copy-start(f32[2,512,256,8]{2,1,3,0:T(8,128)S(1)} %get-tuple-element.460) | copy-start | bytes 25165828 | tf_op jit(solution)/shard_map/while
  83.3 3.2 %copy-start.1 = (f32[2,512,256,8]{2,1,3,0:T(8,128)}, f32[2,512,256,8]{2,1,3,0:T(8,128)S(1)}, u32[]{:S(2)}) copy-start(f32[2,512,256,8]{2,1,3,0:T(8,128)S(1)} %get-tuple-element.460) | copy-start | bytes 25165828 | tf_op jit(solution)/shard_map/while
  95.6 3.2 %copy-start.1 = (f32[2,512,256,8]{2,1,3,0:T(8,128)}, f32[2,512,256,8]{2,1,3,0:T(8,128)S(1)}, u32[]{:S(2)}) copy-start(f32[2,512,256,8]{2,1,3,0:T(8,128)S(1)} %get-tuple-element.460) | copy-start | bytes 25165828 | tf_op jit(solution)/shard_map/while
  107.9 3.2 %copy-start.1 = (f32[2,512,256,8]{2,1,3,0:T(8,128)}, f32[2,512,256,8]{2,1,3,0:T(8,128)S(1)}, u32[]{:S(2)}) copy-start(f32[2,512,256,8]{2,1,3,0:T(8,128)S(1)} %get-tuple-element.460) | copy-start | bytes 25165828 | tf_op jit(solution)/shard_map/while
  119.1 1.7 copy-start.2
  124.4 4.6 %copy-start.5 = (bf16[256,2048]{1,0:T(8,128)(2,1)S(1)}, bf16[256,2048]{1,0:T(8,128)(2,1)}, u32[]{:S(2)}) copy-start(bf16[256,2048]{1,0:T(8,128)(2,1)} %param.13) | copy-start | bytes 3145732
  129.0 75.0 %copy-start.16 = (s32[32]{0:T(128)S(1)}, s32[32]{0:T(128)}, u32[]{:S(2)}) copy-start(s32[32]{0:T(128)} %get-tuple-element.333) | copy-start | bytes 388
  129.0 75.9 %copy-start.12 = (bf16[2048]{0:T(1024)(128)(2,1)S(1)}, bf16[2048]{0:T(1024)(128)(2,1)}, u32[]{:S(2)}) copy-start(bf16[2048]{0:T(1024)(128)(2,1)} %param.20) | copy-start | bytes 12292
  129.0 114.4 %all-gather.7.cloned.1.call-start = ((), (), s32[]{:S(2)}) async-start(), calls=%async_computation.3 | async-start | bytes 1114112 | tf_op jit(solution)/shard_map/all_gather | solution.py:182
  204.0 89.2 %copy-start.6 = (bf16[256,1024]{1,0:T(8,128)(2,1)}, bf16[256,1024]{1,0:T(8,128)(2,1)S(1)}, u32[]{:S(2)}) copy-start(bf16[256,1024]{1,0:T(8,128)(2,1)S(1)} %add_convert_fusion) | copy-start | bytes 1572868
  250.0 43.2 %copy-start.7 = (bf16[32,2048]{1,0:T(8,128)(2,1)}, bf16[32,2048]{1,0:T(8,128)(2,1)S(1)}, u32[]{:S(2)}) copy-start(bf16[32,2048]{1,0:T(8,128)(2,1)S(1)} %fusion.27) | copy-start | bytes 393220
  (4 other events, 2.9 us)
Sparse Core Ops, SparseCore 0:
  10.8 56.5 all-gather.4
  129.1 73.2 reduce-scatter.1
  205.4 37.9 all-gather.6
